TPU v7x, 256 devices: a whole 4x4x8 slice. The times are simulated.
256 devices in a mesh: expert: 16 (over z, core), tensor: 16 (over y, x).
Axes of the slice: x: 4, y: 4, z: 8, core: 2. Of those that a mesh axis runs over, the one named last changes fastest.
Arguments:
- residual_in: bfloat16 [22528, 1024], P(('expert', 'tensor')), may hold values from -6 to 6
- attn_heads: bfloat16 [1024, 22528], P('tensor', 'expert'), may hold values from -6 to 6
- out_proj: bfloat16 [1024, 1024], P('tensor'), may hold values from -0.1875 to 0.1875
- gain_first: float32 [1024], replicated, may hold values from 0.25 to 1.75
- router_weight: float32 [1024, 16], replicated, may hold values from -0.046875 to 0.046875
- routes: int32 [22528, 2], P(('expert', 'tensor')), may hold values from 0 to 15, all different within a row; in each aligned block of 88 rows (0 to 87, 88 to 175, ...) at most 22 rows name the same one
- w_gate: bfloat16 [16, 2816, 1024], P('expert', 'tensor'), may hold values from -0.1875 to 0.1875
- w_upward: bfloat16 [16, 2816, 1024], P('expert', 'tensor'), may hold values from -0.1875 to 0.1875
- w_downward: bfloat16 [16, 2816, 1024], P('expert', 'tensor'), may hold values from -0.21875 to 0.21875
- gain_second: float32 [1024], replicated, may hold values from 0.25 to 1.75
Outputs:
- residual_out: bfloat16 [22528, 1024], P(('expert', 'tensor'))
- next_normed: bfloat16 [22528, 1024], P(('expert', 'tensor'))
Inputs may be any that keep to these rules, and one draw needn't show every extreme that they name: `routes`: each row names two different experts; among the rows of one device no expert is named more than 22 times, and some expert reaches 22.
All inputs are finite; a program needn't handle non-finite values.
Results may differ from a plain program's by a relative error of at most 0.012.
Values may be sent and summed in bfloat16 or wider, within the bound.
No kernel may reach another device: no remote copies, remote signals or barrier semaphores. Data moves between devices by JAX's collectives and lax.ppermute only.
A program may use at most 128 MiB of HBM per device.

v0:
```python
import math
import jax
import jax.numpy as jnp
from jax import lax
from jax.sharding import Mesh
from jax.sharding import PartitionSpec as P

ROWS_AXES = ("expert", "ty", "tx")
TENSOR_AXES = ("ty", "tx")


def rms_scale(values, gain):
    wide = values.astype(jnp.float32)
    scale = lax.rsqrt(jnp.mean(wide * wide, axis=-1, keepdims=True) + 1e-06)
    return (wide * scale * gain).astype(jnp.bfloat16)


def expert_block(inputs, gate_rows, up_rows, down_rows):
    gate_part = lax.dot_general(
        inputs, gate_rows, (((1,), (1,)), ((), ())), preferred_element_type=jnp.float32
    )
    up_part = lax.dot_general(
        inputs, up_rows, (((1,), (1,)), ((), ())), preferred_element_type=jnp.float32
    )
    hid = (jax.nn.gelu(gate_part, approximate=True) * up_part).astype(jnp.bfloat16)
    return jnp.dot(hid, down_rows, preferred_element_type=jnp.float32)


def per_device(
    residual_in,
    attn_heads,
    out_proj,
    gain_first,
    router_weight,
    routes,
    w_gate,
    w_upward,
    w_downward,
    gain_second,
):
    row_count = residual_in.shape[0]
    width = residual_in.shape[1]
    n_expert = lax.axis_size("expert")
    capacity = 4 * row_count // n_expert
    core = lax.axis_index("expert") % 2
    half = width // 2
    my_cols = lax.dynamic_slice_in_dim(out_proj, core * half, half, axis=1)
    my_half = lax.all_gather(my_cols, TENSOR_AXES, axis=0, tiled=True)
    other_half = lax.ppermute(my_half, "expert", [(i, i ^ 1) for i in range(n_expert)])
    own_heads = lax.all_to_all(attn_heads, TENSOR_AXES, 1, 0, tiled=True)
    contract = (((0,), (0,)), ((), ()))
    proj_mine = lax.dot_general(own_heads, my_half, contract, preferred_element_type=jnp.float32)
    proj_other = lax.dot_general(
        own_heads, other_half, contract, preferred_element_type=jnp.float32
    )
    projected = jnp.where(
        core == 0,
        jnp.concatenate([proj_mine, proj_other], axis=1),
        jnp.concatenate([proj_other, proj_mine], axis=1),
    )
    stacked = jnp.concatenate([w_gate, w_upward, w_downward], axis=0)
    n_tx = lax.axis_size("tx")
    pieces = [stacked]
    for shift in range(1, n_tx):
        pieces.append(lax.ppermute(stacked, "tx", [(i, (i + shift) % n_tx) for i in range(n_tx)]))
    hidden_one = (residual_in.astype(jnp.float32) + projected).astype(jnp.bfloat16)
    normed = rms_scale(hidden_one, gain_first)
    logits = jnp.dot(normed.astype(jnp.float32), router_weight, precision=lax.Precision.HIGHEST)
    router_probs = jax.nn.softmax(logits, axis=-1)
    picked = jnp.take_along_axis(router_probs, routes, axis=1)
    gate_weights = picked / jnp.sum(picked, axis=1, keepdims=True)
    flat_ids = routes.reshape(-1)
    expert_iota = jnp.arange(n_expert, dtype=jnp.int32)
    onehot = (flat_ids[:, None] == expert_iota[None, :]).astype(jnp.int32)
    earlier = jnp.cumsum(onehot, axis=0) - onehot
    slot_index = jnp.sum(earlier * onehot, axis=1)
    target = flat_ids * capacity + slot_index
    slot_iota = jnp.arange(n_expert * capacity, dtype=jnp.int32)
    placing = (slot_iota[:, None] == target[None, :]).astype(jnp.bfloat16)
    repeated = jnp.repeat(normed, 2, axis=0)
    send_slots = jnp.dot(placing, repeated, preferred_element_type=jnp.float32).astype(jnp.bfloat16)
    send_slots = send_slots.reshape(n_expert, capacity, width)
    send_slots, *pieces = lax.optimization_barrier((send_slots, *pieces))
    weights = jnp.concatenate(pieces, axis=1)
    gate_rows, up_rows, down_rows = (weights[0], weights[1], weights[2])
    received = lax.all_to_all(send_slots, "expert", split_axis=0, concat_axis=0, tiled=True)
    slot_total = n_expert * capacity
    rows_in = received.reshape(slot_total, width)
    all_rows = lax.all_gather(rows_in, "ty", axis=0, tiled=True)
    expert_sum = lax.psum_scatter(
        expert_block(all_rows, gate_rows, up_rows, down_rows).astype(jnp.bfloat16),
        "ty",
        scatter_dimension=0,
        tiled=True,
    )
    expert_out = expert_sum.reshape(n_expert, capacity, width)
    returned = lax.all_to_all(expert_out, "expert", split_axis=0, concat_axis=0, tiled=True)
    returned = returned.reshape(slot_total, width)
    per_route = lax.dot_general(
        placing, returned, (((0,), (0,)), ((), ())), preferred_element_type=jnp.float32
    )
    per_route = per_route.reshape(row_count, 2, width)
    mixed = jnp.sum(gate_weights[:, :, None] * per_route, axis=1)
    residual_out = (hidden_one.astype(jnp.float32) + mixed).astype(jnp.bfloat16)
    next_normed = rms_scale(residual_out, gain_second)
    return (residual_out, next_normed)


def split_tensor(n):
    inner = int(math.isqrt(n))
    while n % inner:
        inner -= 1
    return (n // inner, inner)


def solution(mesh):
    n_expert = mesh.shape["expert"]
    n_ty, n_tx = split_tensor(mesh.shape["tensor"])
    grid = Mesh(mesh.devices.reshape(n_expert, n_ty, n_tx), ROWS_AXES)
    rows = P(ROWS_AXES, None)
    placed = (
        rows,
        P(TENSOR_AXES, "expert"),
        P(TENSOR_AXES, None),
        P(),
        P(),
        rows,
        P("expert", TENSOR_AXES, None),
        P("expert", TENSOR_AXES, None),
        P("expert", TENSOR_AXES, None),
        P(),
    )
    return jax.shard_map(
        per_device, mesh=grid, in_specs=placed, out_specs=(rows, rows), check_vma=False
    )
```

profile of v0, /device:TPU:1, one launch (start us, length us, event | category | flops | bytes accessed | tf_op | source)
XLA Modules:
  0.0 260.6 jit_solution(8388557563514807960)
XLA Ops:
  7.2 0.0 copy-start
  7.2 0.0 all-gather.3.cloned.1.call-start
  7.3 0.8 copy-done
  8.1 0.6 constant_dynamic-slice_fusion
  8.7 0.0 all-gather.3.cloned.1.call-update
  8.7 1.0 constant_dynamic-update-slice_fusion.2
  9.7 1.0 constant_dynamic-update-slice_fusion.1
  10.8 1.0 constant_dynamic-update-slice_fusion
  11.8 2.1 collective-permute-start.1
  13.9 2.5 collective-permute-start.2
  16.3 1.2 collective-permute-start.3
  17.5 1.4 all_to_all.20
  18.9 0.8 copy.23
  19.7 4.3 %all-to-all-start = ((bf16[64,16,88]{2,0,1:T(8,128)(2,1)}), bf16[64,16,88]{2,0,1:T(8,128)(2,1)S(1)}, u32[]{:S(2)}, u32[]{:S(2)}) async-start(bf16[64,16,88]{2,0,1:T(8,128)(2,1)} %copy.23), calls=%async_computation | async-start | bytes 524288 | tf_op jit(solution)/shard_map/all_to_all | solution.py:50
  24.0 0.0 all-gather.5.cloned.1.call-start
  24.1 0.8 copy.26
  24.9 0.1 reshape.112
  25.0 66.8 %all-gather.3.cloned.1.call-done = bf16[1024,512]{1,0:T(8,128)(2,1)} async-done(((bf16[64,512]{1,0:T(8,128)(2,1)}), bf16[1024,512]{1,0:T(8,128)(2,1)}) %all-gather.3.cloned.1.call-update) | async-done | bytes 1048592 | tf_op jit(solution)/shard_map/all_gather | solution.py:48
  91.8 2.4 collective-permute-start
  94.2 0.6 reduce-window.6
  94.8 0.2 slice_reduce_fusion
  95.0 0.1 bitcast_bitcast_fusion
  95.2 0.0 all-to-all-done
  95.2 1.6 convolution_bitcast_fusion.1
  96.7 0.0 collective-permute-done
  96.7 0.3 convolution_bitcast_fusion
  97.1 0.2 fusion.14
  97.3 0.1 fusion.16
  97.4 0.2 broadcast_in_dim.7
  97.6 0.1 reshape.115
  97.7 0.3 convolution_convert_fusion.1
  98.1 0.2 reshape.116
  98.3 0.0 collective-permute-done.1
  98.3 0.0 collective-permute-done.2
  98.3 0.0 collective-permute-done.3
  98.3 30.0 %all_to_all.29 = bf16[16,22,1024]{2,1,0:T(8,128)(2,1)S(1)} all-to-all(bf16[16,22,1024]{2,1,0:T(8,128)(2,1)S(1)} %reshape.116), channel_id=1, replica_groups=mesh['expert'=16,'ty'=4,'tx'=4] {'expert'}, dimensions={0} | all-to-all | bytes 1441792 | tf_op jit(solution)/shard_map/all_to_all | solution.py:86
  128.3 1.1 reshape.117
  129.4 0.0 all-gather.5.cloned.1.call-update
  129.4 0.2 reduce-scatter.2.cloned.1.call-start
  129.6 1.1 constant_dynamic-update-slice_fusion.6
  130.7 2.3 constant_dynamic-update-slice_fusion.5
  133.0 2.3 constant_dynamic-update-slice_fusion.4
  135.3 2.4 constant_dynamic-update-slice_fusion.3
  137.6 26.3 %all-gather.5.cloned.1.call-done = bf16[1408,1024]{1,0:T(8,128)(2,1)} async-done(((bf16[352,1024]{1,0:T(8,128)(2,1)}), bf16[1408,1024]{1,0:T(8,128)(2,1)}) %all-gather.5.cloned.1.call-update) | async-done | bytes 2883600 | tf_op jit(solution)/shard_map/all_gather | solution.py:89
  164.0 6.6 %fusion.9 = f32[1408,704]{0,1:T(8,128)} fusion(bf16[1408,1024]{1,0:T(8,128)(2,1)} %all-gather.5.cloned.1.call-done, bf16[3,704,1024]{2,1,0:T(8,128)(2,1)} %constant_dynamic-update-slice_fusion.3), kind=kOutput, calls=%fused_computation.15 | convolution fusion | flops 2030043136 | bytes 8290304 | tf_op jit(solution)/shard_map/dot_general | solution.py:19
  170.5 10.3 %convolution_convert_fusion = bf16[1408,1024]{1,0:T(8,128)(2,1)} fusion(bf16[3,704,1024]{2,1,0:T(8,128)(2,1)} %constant_dynamic-update-slice_fusion.3, f32[1408,704]{0,1:T(8,128)} %fusion.9, bf16[1408,1024]{1,0:T(8,128)(2,1)} %all-gather.5.cloned.1.call-done), kind=kOutput, calls=%fused_computation.11 | convolution fusion | flops 4071440384 | bytes 12615680 | tf_op jit(solution)/shard_map/dot_general | solution.py:26
  180.8 0.0 reduce-scatter.2.cloned.1.call-update
  180.9 39.1 %reduce-scatter.2.cloned.1.call-done = bf16[352,1024]{1,0:T(8,128)(2,1)} async-done(((bf16[1408,1024]{1,0:T(8,128)(2,1)}), bf16[352,1024]{1,0:T(8,128)(2,1)}) %reduce-scatter.2.cloned.1.call-update) | async-done | bytes 720912 | tf_op jit(solution)/shard_map/reduce_scatter | solution.py:90
  220.0 2.1 reshape.118
  222.1 7.8 %all-to-all-start.2 = ((bf16[16,22,1024]{2,1,0:T(8,128)(2,1)}), bf16[16,22,1024]{2,1,0:T(8,128)(2,1)S(1)}, u32[]{:S(2)}, u32[]{:S(2)}) async-start(bf16[16,22,1024]{2,1,0:T(8,128)(2,1)} %reshape.118), calls=%async_computation.3 | async-start | bytes 1572864 | tf_op jit(solution)/shard_map/all_to_all | solution.py:97
  229.8 0.1 copy.24
  229.9 0.1 reshape.121
  230.1 0.1 iota_compare_fusion.2
  230.2 0.1 eq.63
  230.3 0.3 fusion.33
  230.6 0.0 copy-start.6
  230.6 2.3 gather_fusion
  232.9 0.1 reshape.124
  233.0 0.1 copy.25
  233.2 19.4 %all-to-all-done.2 = bf16[16,22,1024]{2,1,0:T(8,128)(2,1)S(1)} async-done(((bf16[16,22,1024]{2,1,0:T(8,128)(2,1)}), bf16[16,22,1024]{2,1,0:T(8,128)(2,1)S(1)}, u32[]{:S(2)}, u32[]{:S(2)}) %all-to-all-start.2) | async-done | bytes 720928 | tf_op jit(solution)/shard_map/all_to_all | solution.py:97
  252.5 0.2 reshape.132
  252.8 0.4 fusion.10
  253.1 0.2 fusion.11
  253.3 0.8 fusion.13
  (24 shorter events, 0.2 us)
Async XLA Ops:
  7.2 0.9 copy-start
  7.2 89.9 %copy-start.2 = (bf16[88,1024]{1,0:T(8,128)(2,1)S(1)}, bf16[88,1024]{1,0:T(8,128)(2,1)}, u32[]{:S(2)}) copy-start(bf16[88,1024]{1,0:T(8,128)(2,1)} %param.10) | copy-start | bytes 540676
  7.2 90.1 %copy-start.5 = (f32[1024]{0:T(1024)S(1)}, f32[1024]{0:T(1024)}, u32[]{:S(2)}) copy-start(f32[1024]{0:T(1024)} %param.13) | copy-start | bytes 12292
  7.2 84.6 %all-gather.3.cloned.1.call-start = ((), (), s32[]{:S(2)}) async-start(), calls=%async_computation.4 | async-start | bytes 1114112 | tf_op jit(solution)/shard_map/all_gather | solution.py:48
  11.8 86.5 %collective-permute-start.1 = (bf16[3,176,1024]{2,1,0:T(8,128)(2,1)S(1)}, bf16[3,176,1024]{2,1,0:T(8,128)(2,1)}, u32[]{:S(2)}, u32[]{:S(2)}) collective-permute-start(bf16[3,176,1024]{2,1,0:T(8,128)(2,1)S(1)} %constant_dynamic-update-slice_fusion), channel_id=1, source_target_pairs={{0,1},{1,2},{2,3},{3,0},{4,5},{5,6},{6,7},{7,4},{8,9},{9,10},{10,1... | collective-permute-start | bytes 3244040 | tf_op jit(solution)/shard_map/ppermute | solution.py:65
  13.9 84.4 %collective-permute-start.2 = (bf16[3,176,1024]{2,1,0:T(8,128)(2,1)S(1)}, bf16[3,176,1024]{2,1,0:T(8,128)(2,1)}, u32[]{:S(2)}, u32[]{:S(2)}) collective-permute-start(bf16[3,176,1024]{2,1,0:T(8,128)(2,1)S(1)} %constant_dynamic-update-slice_fusion), channel_id=1, source_target_pairs={{0,2},{1,3},{2,0},{3,1},{4,6},{5,7},{6,4},{7,5},{8,10},{9,11},{10,... | collective-permute-start | bytes 3244040 | tf_op jit(solution)/shard_map/ppermute | solution.py:65
  16.3 82.0 %collective-permute-start.3 = (bf16[3,176,1024]{2,1,0:T(8,128)(2,1)S(1)}, bf16[3,176,1024]{2,1,0:T(8,128)(2,1)}, u32[]{:S(2)}, u32[]{:S(2)}) collective-permute-start(bf16[3,176,1024]{2,1,0:T(8,128)(2,1)S(1)} %constant_dynamic-update-slice_fusion), channel_id=1, source_target_pairs={{0,3},{1,0},{2,1},{3,2},{4,7},{5,4},{6,5},{7,6},{8,11},{9,8},{10,9... | collective-permute-start | bytes 3244040 | tf_op jit(solution)/shard_map/ppermute | solution.py:65
  19.7 75.5 %all-to-all-start = ((bf16[64,16,88]{2,0,1:T(8,128)(2,1)}), bf16[64,16,88]{2,0,1:T(8,128)(2,1)S(1)}, u32[]{:S(2)}, u32[]{:S(2)}) async-start(bf16[64,16,88]{2,0,1:T(8,128)(2,1)} %copy.23), calls=%async_computation | async-start | bytes 524288 | tf_op jit(solution)/shard_map/all_to_all | solution.py:50
  24.0 140.0 %all-gather.5.cloned.1.call-start = ((), (), s32[]{:S(2)}) async-start(), calls=%async_computation.5 | async-start | bytes 3604480 | tf_op jit(solution)/shard_map/all_gather | solution.py:89
  91.8 4.9 %collective-permute-start = (bf16[1024,512]{1,0:T(8,128)(2,1)}, bf16[1024,512]{1,0:T(8,128)(2,1)S(1)}, u32[]{:S(2)}, u32[]{:S(2)}) collective-permute-start(bf16[1024,512]{1,0:T(8,128)(2,1)} %all-gather.3.cloned.1.call-done), channel_id=1, source_target_pairs={{0,16},{16,0},{32,48},{48,32},{64,80},{80,64},{96,112},{112,96},{1... | collective-permute-start | bytes 3145736 | tf_op jit(solution)/shard_map/ppermute | solution.py:49
  129.4 90.6 %reduce-scatter.2.cloned.1.call-start = ((), (), s32[]{:S(2)}) async-start(), calls=%async_computation.6 | async-start | bytes 3604480 | tf_op jit(solution)/shard_map/reduce_scatter | solution.py:90
  180.8 49.0 %copy-start.4 = (s32[88,2]{0,1:T(2,128)S(1)}, s32[88,2]{0,1:T(2,128)}, u32[]{:S(2)}) copy-start(s32[88,2]{0,1:T(2,128)} %param.15) | copy-start | bytes 2116
  180.8 49.5 %copy-start.3 = (f32[1024,16]{0,1:T(8,128)S(1)}, f32[1024,16]{0,1:T(8,128)}, u32[]{:S(2)}) copy-start(f32[1024,16]{0,1:T(8,128)} %param.14) | copy-start | bytes 196612
  222.1 30.5 %all-to-all-start.2 = ((bf16[16,22,1024]{2,1,0:T(8,128)(2,1)}), bf16[16,22,1024]{2,1,0:T(8,128)(2,1)S(1)}, u32[]{:S(2)}, u32[]{:S(2)}) async-start(bf16[16,22,1024]{2,1,0:T(8,128)(2,1)} %reshape.118), calls=%async_computation.3 | async-start | bytes 1572864 | tf_op jit(solution)/shard_map/all_to_all | solution.py:97
  230.6 22.7 %copy-start.6 = (f32[1024]{0:T(1024)S(1)}, f32[1024]{0:T(1024)}, u32[]{:S(2)}) copy-start(f32[1024]{0:T(1024)} %param.19) | copy-start | bytes 12292
  253.3 0.8 copy-start.1
Sparse Core Ops, SparseCore 0:
  11.0 80.7 all-gather.2
  129.5 34.4 all-gather.4
  181.0 38.9 reduce-scatter.1
where the time goes:
time: 261 us
  waiting for transfers between devices  152 us (58%)
  blocking collectives  30 us (11%)
  local copies, waits for them, and re-layouts  22.5 us (9%)
  starting transfers between devices  20.5 us (8%)
  matrix products  19.7 us (8%)
  between operations  14 us (5%)
    all_gather x1, waiting for transfers between devices, per_device(): my_half = lax.all_gather(my_cols, TENSOR_AXES, axis=0, tiled=True)  66.8 us
    reduce_scatter x1, waiting for transfers between devices, per_device(): lax.psum_scatter(expert_block(all_rows, gate_rows, up_rows, down_rows).as...  39.1 us
    all_to_all x1, blocking collectives, per_device(): lax.all_to_all(send_slots, 'expert', split_axis=0, concat_axis=0, tiled=T...  30 us
    all_gather x1, waiting for transfers between devices, per_device(): all_rows = lax.all_gather(rows_in, 'ty', axis=0, tiled=True)  26.3 us
    all_to_all x1, waiting for transfers between devices, per_device(): lax.all_to_all(expert_out, 'expert', split_axis=0, concat_axis=0, tiled=T...  19.4 us
    dot_general x1, matrix products, expert_block(): return jnp.dot(hid, down_rows, preferred_element_type=jnp.float32)  10.3 us
    unnamed x20, local copies, waits for them, and re-layouts  9.27 us
    all_to_all x1, starting transfers between devices, per_device(): lax.all_to_all(expert_out, 'expert', split_axis=0, concat_axis=0, tiled=T...  7.76 us
  transfers between devices with their start and end apart: 9, of which 4 were waited for; matrix products, arithmetic and copies ran while one was open for 8% of the time, Pallas kernels for 0%

commit v1 on v0

--- a/solution.py
+++ b/solution.py
@@ -45,7 +45,9 @@
     core = lax.axis_index("expert") % 2
     half = width // 2
     my_cols = lax.dynamic_slice_in_dim(out_proj, core * half, half, axis=1)
-    my_half = lax.all_gather(my_cols, TENSOR_AXES, axis=0, tiled=True)
+    my_half = jnp.concatenate(
+        lax.all_to_all(jnp.stack([my_cols] * lax.axis_size(TENSOR_AXES)), TENSOR_AXES, 0, 0), axis=0
+    )
     other_half = lax.ppermute(my_half, "expert", [(i, i ^ 1) for i in range(n_expert)])
     own_heads = lax.all_to_all(attn_heads, TENSOR_AXES, 1, 0, tiled=True)
     contract = (((0,), (0,)), ((), ()))

time: 261 us -> 250 us (0.958)
  waiting for transfers between devices: 152 us -> 114 us
  starting transfers between devices: 20.5 us -> 47 us
  local copies, waits for them, and re-layouts: 22.5 us -> 19.4 us
  blocking collectives: 30 us -> 32.9 us
    all_gather x1 -> x0, waiting for transfers between devices: 66.8 us -> none  [per_device(): my_half = lax.all_gather(my_cols, TENSOR_AXES, axis=0, tiled=True)]
    all_to_all x1, waiting for transfers between devices: 0.01 us -> 22.2 us  [per_device(): own_heads = lax.all_to_all(attn_heads, TENSOR_AXES, 1, 0, tiled=True)]
    ppermute x1, starting transfers between devices: 2.44 us -> 22.1 us  [per_device(): lax.ppermute(my_half, 'expert', [(i, i ^ 1) for i in range(n_expert)])]
    all_to_all x0 -> x1, waiting for transfers between devices: none -> 8.37 us  [per_device(): lax.all_to_all(jnp.stack([my_cols] * lax.axis_size(TENSOR_AXES)), TENSOR_...]
    all_to_all x0 -> x1, starting transfers between devices: none -> 7.7 us  [per_device(): lax.all_to_all(jnp.stack([my_cols] * lax.axis_size(TENSOR_AXES)), TENSOR_...]
    all_to_all x1, blocking collectives: 30 us -> 32.9 us  [per_device(): lax.all_to_all(send_slots, 'expert', split_axis=0, concat_axis=0, tiled=T...]
    unnamed x20 -> x26, local copies, waits for them, and re-layouts: 9.27 us -> 7.67 us
  transfers between devices with their start and end apart: 9 -> 9, of which waited for: 4 -> 5; matrix products, arithmetic and copies ran while one was open for 8% -> 7% of each run, Pallas kernels for 0% -> 0%
where the time goes in v1:
time: 250 us
  waiting for transfers between devices  114 us (46%)
  starting transfers between devices  47 us (19%)
  blocking collectives  32.9 us (13%)
  matrix products  19.7 us (8%)
  local copies, waits for them, and re-layouts  19.4 us (8%)
  between operations  14.4 us (6%)
    reduce_scatter x1, waiting for transfers between devices, per_device(): lax.psum_scatter(expert_block(all_rows, gate_rows, up_rows, down_rows).as...  39.1 us
    all_to_all x1, blocking collectives, per_device(): lax.all_to_all(send_slots, 'expert', split_axis=0, concat_axis=0, tiled=T...  32.9 us
    all_gather x1, waiting for transfers between devices, per_device(): all_rows = lax.all_gather(rows_in, 'ty', axis=0, tiled=True)  25 us
    all_to_all x1, waiting for transfers between devices, per_device(): own_heads = lax.all_to_all(attn_heads, TENSOR_AXES, 1, 0, tiled=True)  22.2 us
    ppermute x1, starting transfers between devices, per_device(): lax.ppermute(my_half, 'expert', [(i, i ^ 1) for i in range(n_expert)])  22.1 us
    all_to_all x1, waiting for transfers between devices, per_device(): lax.all_to_all(expert_out, 'expert', split_axis=0, concat_axis=0, tiled=T...  19.4 us
    dot_general x1, matrix products, expert_block(): return jnp.dot(hid, down_rows, preferred_element_type=jnp.float32)  10.3 us
    all_to_all x1, waiting for transfers between devices, per_device(): lax.all_to_all(jnp.stack([my_cols] * lax.axis_size(TENSOR_AXES)), TENSOR_...  8.37 us
  transfers between devices with their start and end apart: 9, of which 5 were waited for; matrix products, arithmetic and copies ran while one was open for 7% of the time, Pallas kernels for 0%

profile of v1, /device:TPU:1, one launch (start us, length us, event | category | flops | bytes accessed | tf_op | source)
XLA Modules:
  0.0 249.7 jit_solution(69897519057126350)
XLA Ops:
  7.2 0.0 copy-start
  7.2 0.8 copy-done
  8.1 1.1 stack.2
  9.2 7.7 %all-to-all-start = ((bf16[16,64,512]{2,1,0:T(8,128)(2,1)}), bf16[16,64,512]{2,1,0:T(8,128)(2,1)S(1)}, u32[]{:S(2)}, u32[]{:S(2)}) async-start(bf16[16,64,512]{2,1,0:T(8,128)(2,1)} %stack.2), calls=%async_computation | async-start | bytes 2097152 | tf_op jit(solution)/shard_map/all_to_all | solution.py:49
  16.9 0.0 copy-start.8
  16.9 1.0 constant_dynamic-update-slice_fusion.2
  18.0 1.4 collective-permute-start.1
  19.4 2.4 collective-permute-start.2
  21.8 1.2 collective-permute-start.3
  23.0 0.5 all_to_all.24
  23.5 0.8 copy.23
  24.3 0.0 copy-done.7
  24.3 0.1 copy.26
  24.4 0.1 reshape.118
  24.6 8.4 %all-to-all-done = bf16[16,64,512]{2,1,0:T(8,128)(2,1)S(1)} async-done(((bf16[16,64,512]{2,1,0:T(8,128)(2,1)}), bf16[16,64,512]{2,1,0:T(8,128)(2,1)S(1)}, u32[]{:S(2)}, u32[]{:S(2)}) %all-to-all-start) | async-done | bytes 1048608 | tf_op jit(solution)/shard_map/all_to_all | solution.py:49
  32.9 4.2 %all-to-all-start.1 = ((bf16[64,16,88]{2,0,1:T(8,128)(2,1)}), bf16[64,16,88]{2,0,1:T(8,128)(2,1)S(1)}, u32[]{:S(2)}, u32[]{:S(2)}) async-start(bf16[64,16,88]{2,0,1:T(8,128)(2,1)} %copy.23), calls=%async_computation.1 | async-start | bytes 524288 | tf_op jit(solution)/shard_map/all_to_all | solution.py:52
  37.1 0.0 all-gather.2.cloned.1.call-start
  37.2 22.1 %collective-permute-start = (bf16[1024,512]{1,0:T(8,128)(2,1)S(1)}, bf16[1024,512]{1,0:T(8,128)(2,1)}, u32[]{:S(2)}, u32[]{:S(2)}) collective-permute-start(bf16[1024,512]{1,0:T(8,128)(2,1)S(1)} %bitcast.48), channel_id=1, source_target_pairs={{0,16},{16,0},{32,48},{48,32},{64,80},{80,64},{96,112},{112,96},{1... | collective-permute-start | bytes 3145736 | tf_op jit(solution)/shard_map/ppermute | solution.py:51
  59.3 0.6 reduce-window.6
  59.9 0.2 slice_reduce_fusion
  60.1 0.1 bitcast_bitcast_fusion
  60.2 22.2 %all-to-all-done.1 = bf16[64,16,88]{2,0,1:T(8,128)(2,1)S(1)} async-done(((bf16[64,16,88]{2,0,1:T(8,128)(2,1)}), bf16[64,16,88]{2,0,1:T(8,128)(2,1)S(1)}, u32[]{:S(2)}, u32[]{:S(2)}) %all-to-all-start.1) | async-done | bytes 180256 | tf_op jit(solution)/shard_map/all_to_all | solution.py:52
  82.4 0.3 convolution_bitcast_fusion.1
  82.8 0.0 collective-permute-done
  82.8 1.6 convolution_bitcast_fusion
  84.3 0.2 fusion.14
  84.5 0.1 fusion.16
  84.6 0.2 broadcast_in_dim.7
  84.8 0.1 reshape.121
  85.0 0.3 convolution_convert_fusion.1
  85.3 0.2 reshape.122
  85.6 0.0 collective-permute-done.1
  85.6 0.0 collective-permute-done.2
  85.6 0.0 collective-permute-done.3
  85.6 32.9 %all_to_all.34 = bf16[16,22,1024]{2,1,0:T(8,128)(2,1)S(1)} all-to-all(bf16[16,22,1024]{2,1,0:T(8,128)(2,1)S(1)} %reshape.122), channel_id=1, replica_groups=mesh['expert'=16,'ty'=4,'tx'=4] {'expert'}, dimensions={0} | all-to-all | bytes 1441792 | tf_op jit(solution)/shard_map/all_to_all | solution.py:88
  118.4 1.1 reshape.123
  119.5 0.0 all-gather.2.cloned.1.call-update
  119.5 0.2 reduce-scatter.2.cloned.1.call-start
  119.8 1.1 constant_dynamic-update-slice_fusion.6
  120.8 2.3 constant_dynamic-update-slice_fusion.5
  123.1 2.3 constant_dynamic-update-slice_fusion.4
  125.4 2.4 constant_dynamic-update-slice_fusion.3
  127.8 25.0 %all-gather.2.cloned.1.call-done = bf16[1408,1024]{1,0:T(8,128)(2,1)} async-done(((bf16[352,1024]{1,0:T(8,128)(2,1)}), bf16[1408,1024]{1,0:T(8,128)(2,1)}) %all-gather.2.cloned.1.call-update) | async-done | bytes 2883600 | tf_op jit(solution)/shard_map/all_gather | solution.py:91
  152.7 6.6 %fusion.9 = f32[1408,704]{0,1:T(8,128)} fusion(bf16[1408,1024]{1,0:T(8,128)(2,1)} %all-gather.2.cloned.1.call-done, bf16[3,704,1024]{2,1,0:T(8,128)(2,1)} %constant_dynamic-update-slice_fusion.3), kind=kOutput, calls=%fused_computation.15 | convolution fusion | flops 2030043136 | bytes 8290304 | tf_op jit(solution)/shard_map/dot_general | solution.py:19
  159.3 10.3 %convolution_convert_fusion = bf16[1408,1024]{1,0:T(8,128)(2,1)} fusion(bf16[3,704,1024]{2,1,0:T(8,128)(2,1)} %constant_dynamic-update-slice_fusion.3, f32[1408,704]{0,1:T(8,128)} %fusion.9, bf16[1408,1024]{1,0:T(8,128)(2,1)} %all-gather.2.cloned.1.call-done), kind=kOutput, calls=%fused_computation.11 | convolution fusion | flops 4071440384 | bytes 12615680 | tf_op jit(solution)/shard_map/dot_general | solution.py:26
  169.6 0.0 reduce-scatter.2.cloned.1.call-update
  169.6 39.1 %reduce-scatter.2.cloned.1.call-done = bf16[352,1024]{1,0:T(8,128)(2,1)} async-done(((bf16[1408,1024]{1,0:T(8,128)(2,1)}), bf16[352,1024]{1,0:T(8,128)(2,1)}) %reduce-scatter.2.cloned.1.call-update) | async-done | bytes 720912 | tf_op jit(solution)/shard_map/reduce_scatter | solution.py:92
  208.7 2.1 reshape.124
  210.8 7.8 %all-to-all-start.3 = ((bf16[16,22,1024]{2,1,0:T(8,128)(2,1)}), bf16[16,22,1024]{2,1,0:T(8,128)(2,1)S(1)}, u32[]{:S(2)}, u32[]{:S(2)}) async-start(bf16[16,22,1024]{2,1,0:T(8,128)(2,1)} %reshape.124), calls=%async_computation.4 | async-start | bytes 1572864 | tf_op jit(solution)/shard_map/all_to_all | solution.py:99
  218.6 0.1 copy.24
  218.7 0.1 reshape.127
  218.8 0.1 iota_compare_fusion.2
  218.9 0.1 eq.63
  219.0 0.0 copy-done.6
  219.0 0.3 fusion.34
  219.4 0.0 copy-start.9
  219.4 2.3 gather_fusion
  221.7 0.1 reshape.130
  221.8 0.1 copy.25
  221.9 19.4 %all-to-all-done.3 = bf16[16,22,1024]{2,1,0:T(8,128)(2,1)S(1)} async-done(((bf16[16,22,1024]{2,1,0:T(8,128)(2,1)}), bf16[16,22,1024]{2,1,0:T(8,128)(2,1)S(1)}, u32[]{:S(2)}, u32[]{:S(2)}) %all-to-all-start.3) | async-done | bytes 720928 | tf_op jit(solution)/shard_map/all_to_all | solution.py:99
  241.3 0.2 reshape.139
  241.5 0.4 fusion.10
  241.9 0.1 fusion.11
  242.0 0.8 fusion.13
  (30 shorter events, 0.3 us)
Async XLA Ops:
  7.2 0.9 copy-start
  7.2 10.7 %copy-start.2 = (bf16[1,176,1024]{2,1,0:T(8,128)(2,1)S(1)}, bf16[1,176,1024]{2,1,0:T(8,128)(2,1)}, u32[]{:S(2)}) copy-start(bf16[1,176,1024]{2,1,0:T(8,128)(2,1)} %param.17) | copy-start | bytes 1081348
  7.2 10.8 %copy-start.3 = (bf16[1,176,1024]{2,1,0:T(8,128)(2,1)S(1)}, bf16[1,176,1024]{2,1,0:T(8,128)(2,1)}, u32[]{:S(2)}) copy-start(bf16[1,176,1024]{2,1,0:T(8,128)(2,1)} %param.18) | copy-start | bytes 1081348
  7.2 15.8 %copy-start.4 = (bf16[64,1408]{1,0:T(8,128)(2,1)S(1)}, bf16[64,1408]{1,0:T(8,128)(2,1)}, u32[]{:S(2)}) copy-start(bf16[64,1408]{1,0:T(8,128)(2,1)} %param.11) | copy-start | bytes 540676
  7.2 17.1 %copy-start.7 = (s32[88,2]{0,1:T(2,128)S(1)}, s32[88,2]{0,1:T(2,128)}, u32[]{:S(2)}) copy-start(s32[88,2]{0,1:T(2,128)} %param.15) | copy-start | bytes 2116
  9.2 75.2 %copy-start.5 = (bf16[88,1024]{1,0:T(8,128)(2,1)S(1)}, bf16[88,1024]{1,0:T(8,128)(2,1)}, u32[]{:S(2)}) copy-start(bf16[88,1024]{1,0:T(8,128)(2,1)} %param.10) | copy-start | bytes 540676
  9.2 23.8 %all-to-all-start = ((bf16[16,64,512]{2,1,0:T(8,128)(2,1)}), bf16[16,64,512]{2,1,0:T(8,128)(2,1)S(1)}, u32[]{:S(2)}, u32[]{:S(2)}) async-start(bf16[16,64,512]{2,1,0:T(8,128)(2,1)} %stack.2), calls=%async_computation | async-start | bytes 2097152 | tf_op jit(solution)/shard_map/all_to_all | solution.py:49
  16.9 67.6 %copy-start.8 = (f32[1024]{0:T(1024)S(1)}, f32[1024]{0:T(1024)}, u32[]{:S(2)}) copy-start(f32[1024]{0:T(1024)} %param.13) | copy-start | bytes 12292
  18.0 67.5 %collective-permute-start.1 = (bf16[3,176,1024]{2,1,0:T(8,128)(2,1)S(1)}, bf16[3,176,1024]{2,1,0:T(8,128)(2,1)}, u32[]{:S(2)}, u32[]{:S(2)}) collective-permute-start(bf16[3,176,1024]{2,1,0:T(8,128)(2,1)S(1)} %constant_dynamic-update-slice_fusion), channel_id=1, source_target_pairs={{0,1},{1,2},{2,3},{3,0},{4,5},{5,6},{6,7},{7,4},{8,9},{9,10},{10,1... | collective-permute-start | bytes 3244040 | tf_op jit(solution)/shard_map/ppermute | solution.py:67
  19.4 66.1 %collective-permute-start.2 = (bf16[3,176,1024]{2,1,0:T(8,128)(2,1)S(1)}, bf16[3,176,1024]{2,1,0:T(8,128)(2,1)}, u32[]{:S(2)}, u32[]{:S(2)}) collective-permute-start(bf16[3,176,1024]{2,1,0:T(8,128)(2,1)S(1)} %constant_dynamic-update-slice_fusion), channel_id=1, source_target_pairs={{0,2},{1,3},{2,0},{3,1},{4,6},{5,7},{6,4},{7,5},{8,10},{9,11},{10,... | collective-permute-start | bytes 3244040 | tf_op jit(solution)/shard_map/ppermute | solution.py:67
  21.8 63.7 %collective-permute-start.3 = (bf16[3,176,1024]{2,1,0:T(8,128)(2,1)S(1)}, bf16[3,176,1024]{2,1,0:T(8,128)(2,1)}, u32[]{:S(2)}, u32[]{:S(2)}) collective-permute-start(bf16[3,176,1024]{2,1,0:T(8,128)(2,1)S(1)} %constant_dynamic-update-slice_fusion), channel_id=1, source_target_pairs={{0,3},{1,0},{2,1},{3,2},{4,7},{5,4},{6,5},{7,6},{8,11},{9,8},{10,9... | collective-permute-start | bytes 3244040 | tf_op jit(solution)/shard_map/ppermute | solution.py:67
  32.9 49.5 %all-to-all-start.1 = ((bf16[64,16,88]{2,0,1:T(8,128)(2,1)}), bf16[64,16,88]{2,0,1:T(8,128)(2,1)S(1)}, u32[]{:S(2)}, u32[]{:S(2)}) async-start(bf16[64,16,88]{2,0,1:T(8,128)(2,1)} %copy.23), calls=%async_computation.1 | async-start | bytes 524288 | tf_op jit(solution)/shard_map/all_to_all | solution.py:52
  37.1 115.6 %all-gather.2.cloned.1.call-start = ((), (), s32[]{:S(2)}) async-start(), calls=%async_computation.5 | async-start | bytes 3604480 | tf_op jit(solution)/shard_map/all_gather | solution.py:91
  37.2 45.6 %collective-permute-start = (bf16[1024,512]{1,0:T(8,128)(2,1)S(1)}, bf16[1024,512]{1,0:T(8,128)(2,1)}, u32[]{:S(2)}, u32[]{:S(2)}) collective-permute-start(bf16[1024,512]{1,0:T(8,128)(2,1)S(1)} %bitcast.48), channel_id=1, source_target_pairs={{0,16},{16,0},{32,48},{48,32},{64,80},{80,64},{96,112},{112,96},{1... | collective-permute-start | bytes 3145736 | tf_op jit(solution)/shard_map/ppermute | solution.py:51
  119.5 89.2 %reduce-scatter.2.cloned.1.call-start = ((), (), s32[]{:S(2)}) async-start(), calls=%async_computation.6 | async-start | bytes 3604480 | tf_op jit(solution)/shard_map/reduce_scatter | solution.py:92
  169.6 49.5 %copy-start.6 = (f32[1024,16]{0,1:T(8,128)S(1)}, f32[1024,16]{0,1:T(8,128)}, u32[]{:S(2)}) copy-start(f32[1024,16]{0,1:T(8,128)} %param.14) | copy-start | bytes 196612
  210.8 30.5 %all-to-all-start.3 = ((bf16[16,22,1024]{2,1,0:T(8,128)(2,1)}), bf16[16,22,1024]{2,1,0:T(8,128)(2,1)S(1)}, u32[]{:S(2)}, u32[]{:S(2)}) async-start(bf16[16,22,1024]{2,1,0:T(8,128)(2,1)} %reshape.124), calls=%async_computation.4 | async-start | bytes 1572864 | tf_op jit(solution)/shard_map/all_to_all | solution.py:99
  219.4 22.7 %copy-start.9 = (f32[1024]{0:T(1024)S(1)}, f32[1024]{0:T(1024)}, u32[]{:S(2)}) copy-start(f32[1024]{0:T(1024)} %param.19) | copy-start | bytes 12292
  242.0 0.8 copy-start.1
Sparse Core Ops, SparseCore 0:
  119.6 33.0 all-gather.1
  169.7 38.9 reduce-scatter.1
